TPU v7x, 256 devices: a whole 4x4x8 slice. The times are simulated.
256 devices in a mesh: req: 4 (over x), seq: 8 (over z_lo, y), tp: 8 (over z_hi, core).
Axes of the slice: x: 4, y: 4, z: 8 (z_hi: 4, z_lo: 2; z = z_hi * 2 + z_lo), core: 2. Of those that a mesh axis runs over, the one named last changes fastest.
Arguments:
- img_hidden: bfloat16 [16384, 3072], P(('req', 'seq'), 'tp'), parts along dimension 0, may hold values from -6 to 6
- txt_hidden: bfloat16 [2048, 3072], P(('req', 'seq'), 'tp'), parts along dimension 0, may hold values from -6 to 6
- img_mod: bfloat16 [12, 3072], P('req'), parts along dimension 0, may hold values from -3 to 3
- txt_mod: bfloat16 [12, 3072], P('req'), parts along dimension 0, may hold values from -3 to 3
- img_qkv: bfloat16 [3072, 3, 3072], P('seq', None, 'tp')
- txt_qkv: bfloat16 [3072, 3, 3072], P('seq', None, 'tp'), may hold values from -0.109375 to 0.109375
- qk_gains: float32 [4, 128], replicated, may hold values from 0.5 to 4.5, as said below
- img_out_w: bfloat16 [3072, 3072], P('tp', 'seq'), may hold values from -0.109375 to 0.109375
- txt_out_w: bfloat16 [3072, 3072], P('tp', 'seq'), may hold values from -0.109375 to 0.109375
- final_mod: bfloat16 [8, 3072], P('req'), parts along dimension 0, may hold values from -3 to 3
- final_w: bfloat16 [3072, 64], P('tp'), may hold values from -0.109375 to 0.109375
- conv_w: bfloat16 [3, 3, 64, 64], replicated, may hold values from -0.25 to 0.25
- latent: float32 [256, 4096], P(('req', 'seq'), 'tp'), parts along dimension 0, may hold values from -6 to 6
- text_len: int32 [4], P('req'), parts along dimension 0, may hold values from 1 to 512
- step_index: int32 [4], P('req'), parts along dimension 0, may hold values from 0 to 27
Outputs:
- img_next: bfloat16 [16384, 3072], P(('req', 'seq'), 'tp'), parts along dimension 0
- txt_next: bfloat16 [2048, 3072], P(('req', 'seq'), 'tp'), parts along dimension 0
- velocity: float32 [256, 4096], P(('req', 'seq'), 'tp'), parts along dimension 0
- latent_next: float32 [256, 4096], P(('req', 'seq'), 'tp'), parts along dimension 0
- denoised: float32 [256, 4096], P(('req', 'seq'), 'tp'), parts along dimension 0
There are 4 independent parts, one for each index of `req`. A program takes and returns all parts, laid end to end along the dimension named above; an argument that names none is the same for every part. Nothing has to cross between parts.
Inputs may be any that keep to these rules, and one draw needn't show every extreme that they name: `qk_gains`: positive gains.
All inputs are finite; a program needn't handle non-finite values.
Results may differ from a plain program's by a relative error of at most 0.014.
Values may be sent and summed in bfloat16 or wider, within the bound.
No kernel may reach another device: no remote copies, remote signals or barrier semaphores. Data moves between devices by JAX's collectives and lax.ppermute only.
A program may use at most 128 MiB of HBM per device.

v0:
```python
import math
import jax
import jax.numpy as jnp
from jax import lax
from jax.sharding import PartitionSpec as P

STEPS = 28
EPS = 1e-06
SHIFT_MU = 1.15
THETA = 10000.0


def extended(block, sides, width):
    for axis, dim in sides:
        count = lax.axis_size(axis)
        forward = [(i, i + 1) for i in range(count - 1)]
        backward = [(target, source) for source, target in forward]
        low = lax.ppermute(
            lax.slice_in_dim(block, block.shape[dim] - width, None, axis=dim), axis, forward
        )
        high = lax.ppermute(lax.slice_in_dim(block, 0, width, axis=dim), axis, backward)
        block = jnp.concatenate([low, block, high], axis=dim)
    return block


def modulate(hidden, mod_rows):
    values = hidden.astype(jnp.float32)
    mod_f = mod_rows.astype(jnp.float32)
    row_mean = jnp.mean(values, -1, keepdims=True)
    row_var = jnp.mean((values - row_mean) ** 2, -1, keepdims=True)
    normed = (values - row_mean) * lax.rsqrt(row_var + EPS)
    return (normed * (1.0 + mod_f[1]) + mod_f[0]).astype(jnp.bfloat16)


def rms_gain(values, gain_row):
    return values * lax.rsqrt(jnp.mean(values * values, -1, keepdims=True) + EPS) * gain_row


def rope_angles(row_pos, col_pos, head_dim):
    lead = head_dim // 16
    span = 7 * head_dim // 32
    freq = THETA ** (-jnp.arange(span, dtype=jnp.float32) / span)
    zero_part = jnp.zeros((row_pos.shape[0], lead), jnp.float32)
    return jnp.concatenate(
        [zero_part, row_pos[:, None] * freq[None], col_pos[:, None] * freq[None]], 1
    )


def apply_rope(values, angles):
    count, heads_n, head_dim = values.shape
    pairs = values.reshape(count, heads_n, head_dim // 2, 2)
    first = pairs[..., 0]
    second = pairs[..., 1]
    cosine = jnp.cos(angles)[:, None, :]
    sine = jnp.sin(angles)[:, None, :]
    turned = jnp.stack([first * cosine - second * sine, first * sine + second * cosine], -1)
    return turned.reshape(values.shape)


def split_heads(mixed, gain_q, gain_k, angles):
    head_dim = gain_q.shape[0]
    shaped = mixed.reshape(mixed.shape[0], 3, -1, head_dim)
    query = rms_gain(shaped[:, 0], gain_q)
    keyed = rms_gain(shaped[:, 1], gain_k)
    if angles is not None:
        query = apply_rope(query, angles)
        keyed = apply_rope(keyed, angles)
    return (
        query.astype(jnp.bfloat16),
        keyed.astype(jnp.bfloat16),
        shaped[:, 2].astype(jnp.bfloat16),
    )


def noise_level(tval):
    factor = math.exp(SHIFT_MU)
    return factor * tval / (factor * tval + 1.0 - tval)


def add_rows(normed, piece):
    flat_piece = piece.reshape(piece.shape[0], piece.shape[1] * piece.shape[2])
    return jnp.dot(normed, flat_piece, preferred_element_type=jnp.float32)


def per_device(
    img_hidden,
    txt_hidden,
    img_mod,
    txt_mod,
    img_qkv,
    txt_qkv,
    qk_gains,
    img_out_w,
    txt_out_w,
    final_mod,
    final_w,
    conv_w,
    latent,
    text_len,
    step_index,
):
    seq_count = lax.axis_size("seq")
    seq_at = lax.axis_index("seq")
    tp_at = lax.axis_index("tp")
    img_rows = img_hidden.shape[0]
    txt_rows = txt_hidden.shape[0]
    local_width = img_hidden.shape[1]
    img_full, txt_full = (
        lax.all_gather(img_hidden, "tp", axis=1, tiled=True),
        lax.all_gather(txt_hidden, "tp", axis=1, tiled=True),
    )
    full_width = img_full.shape[1]
    img_norm = modulate(img_full, img_mod)
    txt_norm = modulate(txt_full, txt_mod)
    img_mixed = add_rows(img_norm, lax.all_gather(img_qkv, "seq", axis=0, tiled=True))
    txt_norm_rows = lax.all_to_all(txt_norm, "seq", 1, 0, tiled=True)
    txt_mixed = lax.psum_scatter(
        add_rows(txt_norm_rows, txt_qkv), "seq", scatter_dimension=0, tiled=True
    )
    head_dim = qk_gains.shape[1]
    grid_side = latent.shape[0] * seq_count
    token_ids = seq_at * img_rows + jnp.arange(img_rows, dtype=jnp.int32)
    row_pos = (token_ids // grid_side).astype(jnp.float32)
    col_pos = (token_ids % grid_side).astype(jnp.float32)
    angles = rope_angles(row_pos, col_pos, head_dim)
    img_query, img_key, img_value = split_heads(img_mixed, qk_gains[0], qk_gains[1], angles)
    txt_query, txt_key, txt_value = split_heads(txt_mixed, qk_gains[2], qk_gains[3], None)
    local_len = txt_rows + img_rows
    heads_local = img_query.shape[1]
    queries = jnp.concatenate([txt_query, img_query], 0)
    keys_local = jnp.concatenate([txt_key, img_key], 0).reshape(local_len, heads_local * head_dim)
    values_local = jnp.concatenate([txt_value, img_value], 0).reshape(
        local_len, heads_local * head_dim
    )
    limit = text_len[0]
    score_scale = head_dim ** (-0.5)
    start_state = (
        jnp.full((heads_local, local_len), -1e30, jnp.float32),
        jnp.zeros((heads_local, local_len), jnp.float32),
        jnp.zeros((heads_local, local_len, head_dim), jnp.float32),
    )
    key_piece = lax.all_gather(keys_local, "seq", axis=0, tiled=True)
    value_piece = lax.all_gather(values_local, "seq", axis=0, tiled=True)
    blocks = key_piece.shape[0] // local_len

    def advance(block, state):
        peak, running, accum = state
        key_block = lax.dynamic_slice_in_dim(key_piece, block * local_len, local_len, 0).reshape(
            local_len, heads_local, head_dim
        )
        value_block = lax.dynamic_slice_in_dim(
            value_piece, block * local_len, local_len, 0
        ).reshape(local_len, heads_local, head_dim)
        within = jnp.arange(local_len, dtype=jnp.int32)
        text_pos = block * txt_rows + within
        usable = (within >= txt_rows) | (text_pos < limit)
        scores = (
            jnp.einsum("qhd,khd->hqk", queries, key_block, preferred_element_type=jnp.float32)
            * score_scale
        )
        scores = jnp.where(usable[None, None, :], scores, -1e30)
        new_peak = jnp.maximum(peak, jnp.max(scores, -1))
        rescale = jnp.exp(peak - new_peak)
        weights = jnp.exp(scores - new_peak[..., None])
        running = running * rescale + jnp.sum(weights, -1)
        accum = accum * rescale[..., None] + jnp.einsum(
            "hqk,khd->hqd",
            weights.astype(jnp.bfloat16),
            value_block,
            preferred_element_type=jnp.float32,
        )
        return (new_peak, running, accum)

    peak, running, accum = lax.fori_loop(0, blocks, advance, start_state)
    attn = (
        (accum / running[..., None])
        .astype(jnp.bfloat16)
        .transpose(1, 0, 2)
        .reshape(local_len, heads_local * head_dim)
    )
    txt_attn = attn[:txt_rows]
    img_attn = attn[txt_rows:]
    img_term = jnp.dot(
        img_attn,
        lax.all_gather(img_out_w, "seq", axis=1, tiled=True),
        preferred_element_type=jnp.float32,
    )
    txt_term = jnp.dot(
        lax.all_gather(txt_attn, "seq", axis=0, tiled=True),
        txt_out_w,
        preferred_element_type=jnp.float32,
    )
    txt_part = lax.psum_scatter(
        txt_term.astype(jnp.bfloat16).astype(jnp.float32), "tp", scatter_dimension=0, tiled=True
    )
    side = lax.axis_size("tp")
    swap = [(a * side + b, b * side + a) for a in range(side) for b in range(side)]
    txt_out = lax.ppermute(txt_part, ("seq", "tp"), swap)
    img_out = lax.psum_scatter(
        img_term.astype(jnp.bfloat16), "tp", scatter_dimension=1, tiled=True
    ).astype(jnp.float32)
    img_gate = lax.dynamic_slice_in_dim(
        img_mod.astype(jnp.float32)[2], tp_at * local_width, local_width
    )
    txt_gate = lax.dynamic_slice_in_dim(
        txt_mod.astype(jnp.float32)[2], tp_at * local_width, local_width
    )
    img_next = (img_hidden.astype(jnp.float32) + img_gate * img_out).astype(jnp.bfloat16)
    text_valid = seq_at * txt_rows + jnp.arange(txt_rows, dtype=jnp.int32) < limit
    txt_base = txt_hidden.astype(jnp.float32)
    txt_next = jnp.where(text_valid[:, None], txt_base + txt_gate * txt_out, txt_base).astype(
        jnp.bfloat16
    )
    shift_row = lax.dynamic_slice_in_dim(final_mod[0], tp_at * local_width, local_width)
    scale_row = lax.dynamic_slice_in_dim(final_mod[1], tp_at * local_width, local_width)
    final_shift = shift_row.astype(jnp.float32)
    final_scale = scale_row.astype(jnp.float32)
    weight_final = final_w.astype(jnp.float32)
    values = img_next.astype(jnp.float32)
    channels = final_w.shape[1]
    final_gain = 1.0 + final_scale
    high = lax.Precision.HIGHEST
    lifted = jnp.dot(values * final_gain, weight_final, precision=high)
    consts = jnp.stack(
        [
            jnp.dot(final_gain, weight_final, precision=high),
            jnp.dot(final_shift, weight_final, precision=high),
        ]
    )
    packed = jnp.concatenate(
        [
            jnp.concatenate(
                [lifted, jnp.sum(values, -1)[:, None], jnp.sum(values * values, -1)[:, None]], 1
            ),
            jnp.pad(consts, ((0, 0), (0, 2))),
        ],
        0,
    )
    packed = lax.psum(packed, "tp")
    lifted = packed[:img_rows, :channels]
    row_mean = packed[:img_rows, channels] / full_width
    row_var = packed[:img_rows, channels + 1] / full_width - row_mean * row_mean
    row_scale = lax.rsqrt(row_var + EPS)[:, None]
    patch = (
        row_scale * (lifted - row_mean[:, None] * packed[img_rows, :channels])
        + packed[img_rows + 1, :channels]
    )
    band_rows = latent.shape[0]
    patch_band = patch.astype(jnp.bfloat16).reshape(band_rows, grid_side * channels)
    rimmed = extended(patch_band, (("seq", 0),), 1)
    col_width = latent.shape[1] // channels
    framed = jnp.pad(rimmed.reshape(band_rows + 2, grid_side, channels), ((0, 0), (1, 1), (0, 0)))
    window = lax.dynamic_slice_in_dim(framed, tp_at * col_width, col_width + 2, 1)
    velocity = jnp.zeros((band_rows, col_width, channels), jnp.float32)
    for row_shift in range(3):
        for col_shift in range(3):
            velocity = velocity + jnp.einsum(
                "rci,io->rco",
                window[row_shift : row_shift + band_rows, col_shift : col_shift + col_width],
                conv_w[row_shift, col_shift],
                preferred_element_type=jnp.float32,
            )
    velocity_flat = velocity.reshape(band_rows, col_width * channels)
    step_f = step_index[0].astype(jnp.float32)
    t_now = 1.0 - step_f / STEPS
    t_after = 1.0 - (step_f + 1.0) / STEPS
    delta = noise_level(t_after) - noise_level(t_now)
    latent_next = latent + delta * velocity_flat
    denoised = latent - noise_level(t_now) * velocity_flat
    return (img_next, txt_next, velocity_flat, latent_next, denoised)


def solution(mesh):
    placed = (
        P(("req", "seq"), "tp"),
        P(("req", "seq"), "tp"),
        P("req", None),
        P("req", None),
        P("seq", None, "tp"),
        P("seq", None, "tp"),
        P(),
        P("tp", "seq"),
        P("tp", "seq"),
        P("req", None),
        P("tp", None),
        P(),
        P(("req", "seq"), "tp"),
        P("req"),
        P("req"),
    )
    return jax.shard_map(
        per_device,
        mesh=mesh,
        in_specs=placed,
        out_specs=(
            P(("req", "seq"), "tp"),
            P(("req", "seq"), "tp"),
            P(("req", "seq"), "tp"),
            P(("req", "seq"), "tp"),
            P(("req", "seq"), "tp"),
        ),
        check_vma=False,
    )
```

profile of v0, /device:TPU:24, one launch (start us, length us, event | category | flops | bytes accessed | tf_op | source)
XLA Modules:
  0.0 591.8 jit_solution(8181375661822205329)
XLA Ops:
  8.0 1.4 fusion.103
  10.2 18.8 %all_gather.21 = bf16[64,3072]{1,0:T(8,128)(2,1)S(1)} all-gather(bf16[64,384]{1,0:T(8,128)(2,1)} %param.18), channel_id=1, replica_groups=mesh['req'=4,'seq'=8,'tp'=8] {'tp'}, dimensions={1}, use_global_device_ids=true | all-gather | bytes 442368 | tf_op jit(solution)/shard_map/all_gather | solution.py:110
  30.4 5.4 all-to-all-start
  35.8 2.5 copy.106
  38.3 4.1 all-to-all-done
  42.4 2.2 fusion.106
  45.2 2.2 copy.109
  49.9 1.2 fusion.44
  51.8 57.2 %reduce-scatter.6.cloned.1.call-done = f32[64,1152]{1,0:T(8,128)} async-done(((f32[512,1152]{1,0:T(8,128)}), f32[64,1152]{1,0:T(8,128)}) %reduce-scatter.6.cloned.1.call-update) | async-done | bytes 294928 | tf_op jit(solution)/shard_map/reduce_scatter | solution.py:117
  109.0 1.1 reshape.280
  110.8 2.5 convert_reduce_fusion
  115.1 61.8 %all-gather.8.cloned.1.call-done = bf16[3072,3,384]{0,2,1:T(8,128)(2,1)} async-done(((bf16[384,3,384]{0,2,1:T(8,128)(2,1)}), bf16[3072,3,384]{0,2,1:T(8,128)(2,1)}) %all-gather.8.cloned.1.call-update) | async-done | bytes 7077904 | tf_op jit(solution)/shard_map/all_gather | solution.py:115
  176.9 6.4 %fusion.23 = f32[512,3,3,128]{0,3,2,1:T(8,128)S(1)} fusion(bf16[3,3,128,3072]{3,2,1,0:T(8,128)(2,1)} %bitcast.197, bf16[512,3072]{1,0:T(8,128)(2,1)S(1)} %copy-done.1, f32[3072]{0:T(1024)} %bitcast.192, f32[3072]{0:T(1024)S(1)} %bitcast.191, f32[512]{0:T(512)} %add_rsqrt_fusion.5, f32[512]{0:T(512)S(1)} %broadcast_multiply_fusion.2), kind=kOutput, calls=%fused_computation.34 | convolution fusion | flops 3633315840 | bytes 12611584 | tf_op jit(solution)/shard_map/dot_general | solution.py:82
  183.7 1.1 copy-done.5
  186.5 2.1 subtract_convert_fusion
  191.0 1.2 slice.343
  196.1 43.4 %all-gather.10.cloned.1.call-done = bf16[4608,384]{1,0:T(8,128)(2,1)} async-done(((bf16[576,384]{1,0:T(8,128)(2,1)}), bf16[4608,384]{1,0:T(8,128)(2,1)}) %all-gather.10.cloned.1.call-update) | async-done | bytes 3538960 | tf_op jit(solution)/shard_map/all_gather | solution.py:142
  239.5 50.3 %all-gather.12.cloned.1.call-done = bf16[4608,384]{1,0:T(8,128)(2,1)} async-done(((bf16[576,384]{1,0:T(8,128)(2,1)}), bf16[4608,384]{1,0:T(8,128)(2,1)}) %all-gather.12.cloned.1.call-update) | async-done | bytes 3538960 | tf_op jit(solution)/shard_map/all_gather | solution.py:143
  289.8 104.1 %while.18 = (s32[]{:T(128)}, f32[3,576]{1,0:T(4,128)S(1)}, f32[3,576]{1,0:T(4,128)}, f32[3,576,128]{2,1,0:T(8,128)S(1)}, s32[]{:T(128)}, /*index=5*/bf16[4608,38...) while((s32[]{:T(128)}, f32[3,576]{1,0:T(4,128)S(1)}, ...), condition=%wide.region_12.13_spmd.clone, body=%wide.region_9.12_spmd.clone.sunk | while | flops 521231040 | bytes 18747912 | solution.py:174
  289.8 1.2 constant_dynamic-slice_fusion.7
  292.0 3.1 bitcast_reduce_fusion.2
  295.1 3.2 fusion.133
  298.6 4.1 fusion.135
  302.8 1.2 constant_dynamic-slice_fusion.7
  305.0 3.1 bitcast_reduce_fusion.2
  308.1 3.3 fusion.133
  311.7 4.1 fusion.135
  315.9 1.2 constant_dynamic-slice_fusion.7
  318.0 3.1 bitcast_reduce_fusion.2
  321.1 3.2 fusion.133
  324.7 4.2 fusion.135
  328.9 1.3 constant_dynamic-slice_fusion.7
  331.1 3.1 bitcast_reduce_fusion.2
  334.2 3.2 fusion.133
  337.7 4.1 fusion.135
  341.9 1.2 constant_dynamic-slice_fusion.7
  344.1 3.1 bitcast_reduce_fusion.2
  347.2 3.2 fusion.133
  350.7 4.1 fusion.135
  354.9 1.2 constant_dynamic-slice_fusion.7
  357.1 3.1 bitcast_reduce_fusion.2
  360.2 3.2 fusion.133
  363.7 4.1 fusion.135
  367.9 1.2 constant_dynamic-slice_fusion.7
  370.1 3.1 bitcast_reduce_fusion.2
  373.2 3.2 fusion.133
  376.7 4.1 fusion.135
  380.9 1.2 constant_dynamic-slice_fusion.7
  383.1 3.1 bitcast_reduce_fusion.2
  386.2 3.2 fusion.133
  389.7 4.1 fusion.135
  396.7 3.6 convolution_convert_fusion
  400.4 2.8 copy.131
  403.4 31.2 %all_gather.27 = bf16[512,384]{1,0:T(8,128)(2,1)S(1)} all-gather(bf16[64,384]{1,0:T(8,128)(2,1)S(1)} %copy.129), channel_id=1, replica_groups=mesh['req'=4,'seq'=8,'tp'=8] {'seq'}, dimensions={0}, use_global_device_ids=true | all-gather | bytes 442368 | tf_op jit(solution)/shard_map/all_gather | solution.py:189
  434.6 1.3 fusion.29
  437.2 18.4 %reduce-scatter.10.cloned.1.call-done = bf16[384,512]{1,0:T(8,128)(2,1)} async-done(((bf16[3072,512]{1,0:T(8,128)(2,1)}), bf16[384,512]{1,0:T(8,128)(2,1)}) %reduce-scatter.10.cloned.1.call-update) | async-done | bytes 393232
  455.6 1.2 copy.132
  460.6 34.9 %reduce-scatter.8.cloned.1.call-done = f32[64,384]{1,0:T(8,128)} async-done(((f32[512,384]{1,0:T(8,128)}), f32[64,384]{1,0:T(8,128)}) %reduce-scatter.8.cloned.1.call-update) | async-done | bytes 98320 | tf_op jit(solution)/shard_map/reduce_scatter | solution.py:193
  495.5 4.1 collective-permute-start
  499.6 69.3 %all-reduce.4.cloned.1.call-done = f32[514,66]{0,1:T(8,128)} async-done(((f32[514,66]{0,1:T(8,128)}), f32[514,66]{0,1:T(8,128)}) %all-reduce.4.cloned.1.call-update) | async-done | bytes 135712 | tf_op jit(solution)/shard_map/psum | solution.py:239
  569.7 1.0 slice_reduce_fusion.1
  572.0 2.5 collective-permute-start.1
  574.6 3.4 collective-permute-start.2
  579.0 3.4 collective-permute-done.2
  (241 shorter events, 38.1 us)
Async XLA Ops:
  8.0 426.6 %copy-start = (bf16[384,384]{1,0:T(8,128)(2,1)S(1)}, bf16[384,384]{1,0:T(8,128)(2,1)}, u32[]{:S(2)}) copy-start(bf16[384,384]{1,0:T(8,128)(2,1)} %param.25) | copy-start | bytes 884740
  30.4 14.8 %copy-start.8 = (bf16[384,3,384]{2,0,1:T(8,128)(2,1)S(1)}, bf16[384,3,384]{2,0,1:T(8,128)(2,1)}, u32[]{:S(2)}) copy-start(bf16[384,3,384]{2,0,1:T(8,128)(2,1)} %param.21) | copy-start | bytes 2654212
  30.4 11.9 %all-to-all-start = ((bf16[64,8,384]{2,0,1:T(8,128)(2,1)}), bf16[64,8,384]{2,0,1:T(8,128)(2,1)S(1)}, u32[]{:S(2)}, u32[]{:S(2)}) async-start(bf16[64,8,384]{2,0,1:T(8,128)(2,1)} %bitcast.155), calls=%async_computation | async-start | bytes 786432 | tf_op jit(solution)/shard_map/all_to_all | solution.py:116
  35.8 73.2 %reduce-scatter.6.cloned.1.call-start = ((), (), s32[]{:S(2)}) async-start(), calls=%async_computation.4 | async-start | bytes 2654208 | tf_op jit(solution)/shard_map/reduce_scatter | solution.py:117
  42.3 5.3 copy-start.18
  42.3 5.3 copy-start.23
  44.6 66.2 %all-gather.6.cloned.1.call-start = ((), (), s32[]{:S(2)}) async-start(), calls=%async_computation.5 | async-start | bytes 3538944 | tf_op jit(solution)/shard_map/all_gather | solution.py:109
  45.2 131.8 %all-gather.8.cloned.1.call-start = ((), (), s32[]{:S(2)}) async-start(), calls=%async_computation.6 | async-start | bytes 7962624 | tf_op jit(solution)/shard_map/all_gather | solution.py:115
  47.4 192.1 %all-gather.10.cloned.1.call-start = ((), (), s32[]{:S(2)}) async-start(), calls=%async_computation.7 | async-start | bytes 3981312 | tf_op jit(solution)/shard_map/all_gather | solution.py:142
  110.0 0.7 copy-start.3
  110.8 2.8 copy-start.1
  183.4 1.4 copy-start.5
  183.4 2.4 copy-start.17
  183.4 2.7 copy-start.16
  183.4 3.1 copy-start.9
  183.4 3.1 copy-start.10
  186.1 4.8 copy-start.4
  188.6 5.7 copy-start.22
  190.9 98.9 %all-gather.12.cloned.1.call-start = ((), (), s32[]{:S(2)}) async-start(), calls=%async_computation.8 | async-start | bytes 3981312 | tf_op jit(solution)/shard_map/all_gather | solution.py:143
  193.2 203.5 %all-gather.14.cloned.1.call-start = ((), (), s32[]{:S(2)}) async-start(), calls=%async_computation.9 | async-start | bytes 2654208 | tf_op jit(solution)/shard_map/all_gather | solution.py:185
  193.8 261.8 %reduce-scatter.10.cloned.1.call-start = ((), (), s32[]{:S(2)}) async-start(), calls=%async_computation.12 | async-start | bytes 3538944
  291.9 6.4 %copy-start.12 = (f32[3,576]{1,0:T(4,128)S(1)}, f32[3,576]{1,0:T(4,128)}, u32[]{:S(2)}) copy-start(f32[3,576]{1,0:T(4,128)} %get-tuple-element.355) | copy-start | bytes 20740 | tf_op jit(solution)/shard_map/while
  298.3 4.4 copy-start.13
  305.0 6.4 %copy-start.12 = (f32[3,576]{1,0:T(4,128)S(1)}, f32[3,576]{1,0:T(4,128)}, u32[]{:S(2)}) copy-start(f32[3,576]{1,0:T(4,128)} %get-tuple-element.355) | copy-start | bytes 20740 | tf_op jit(solution)/shard_map/while
  311.4 4.4 copy-start.13
  318.0 6.4 %copy-start.12 = (f32[3,576]{1,0:T(4,128)S(1)}, f32[3,576]{1,0:T(4,128)}, u32[]{:S(2)}) copy-start(f32[3,576]{1,0:T(4,128)} %get-tuple-element.355) | copy-start | bytes 20740 | tf_op jit(solution)/shard_map/while
  324.4 4.4 copy-start.13
  331.1 6.4 %copy-start.12 = (f32[3,576]{1,0:T(4,128)S(1)}, f32[3,576]{1,0:T(4,128)}, u32[]{:S(2)}) copy-start(f32[3,576]{1,0:T(4,128)} %get-tuple-element.355) | copy-start | bytes 20740 | tf_op jit(solution)/shard_map/while
  337.5 4.4 copy-start.13
  344.1 6.4 %copy-start.12 = (f32[3,576]{1,0:T(4,128)S(1)}, f32[3,576]{1,0:T(4,128)}, u32[]{:S(2)}) copy-start(f32[3,576]{1,0:T(4,128)} %get-tuple-element.355) | copy-start | bytes 20740 | tf_op jit(solution)/shard_map/while
  350.5 4.4 copy-start.13
  357.1 6.4 %copy-start.12 = (f32[3,576]{1,0:T(4,128)S(1)}, f32[3,576]{1,0:T(4,128)}, u32[]{:S(2)}) copy-start(f32[3,576]{1,0:T(4,128)} %get-tuple-element.355) | copy-start | bytes 20740 | tf_op jit(solution)/shard_map/while
  363.5 4.4 copy-start.13
  370.1 6.4 %copy-start.12 = (f32[3,576]{1,0:T(4,128)S(1)}, f32[3,576]{1,0:T(4,128)}, u32[]{:S(2)}) copy-start(f32[3,576]{1,0:T(4,128)} %get-tuple-element.355) | copy-start | bytes 20740 | tf_op jit(solution)/shard_map/while
  376.5 4.4 copy-start.13
  383.1 6.4 %copy-start.12 = (f32[3,576]{1,0:T(4,128)S(1)}, f32[3,576]{1,0:T(4,128)}, u32[]{:S(2)}) copy-start(f32[3,576]{1,0:T(4,128)} %get-tuple-element.355) | copy-start | bytes 20740 | tf_op jit(solution)/shard_map/while
  389.5 4.4 copy-start.13
  395.0 0.8 copy-start.2
  400.3 2.9 slice-start
  403.2 32.8 %copy-start.20 = (bf16[2,3072]{1,0:T(2,128)(2,1)S(1)}, bf16[2,3072]{1,0:T(2,128)(2,1)}, u32[]{:S(2)}) copy-start(bf16[2,3072]{1,0:T(2,128)(2,1)} %param.26) | copy-start | bytes 36868
  403.2 32.9 %copy-start.11 = (bf16[384,64]{0,1:T(8,128)(2,1)S(1)}, bf16[384,64]{0,1:T(8,128)(2,1)}, u32[]{:S(2)}) copy-start(bf16[384,64]{0,1:T(8,128)(2,1)} %param.27) | copy-start | bytes 147460
  403.2 53.7 %copy-start.6 = (bf16[512,384]{1,0:T(8,128)(2,1)S(1)}, bf16[512,384]{1,0:T(8,128)(2,1)}, u32[]{:S(2)}) copy-start(bf16[512,384]{1,0:T(8,128)(2,1)} %param.17) | copy-start | bytes 1179652
  403.2 174.8 %copy-start.14 = (bf16[64,384]{1,0:T(8,128)(2,1)S(1)}, bf16[64,384]{1,0:T(8,128)(2,1)}, u32[]{:S(2)}) copy-start(bf16[64,384]{1,0:T(8,128)(2,1)} %param.18) | copy-start | bytes 147460
  403.2 179.4 %copy-start.15 = (bf16[3,3,64,64]{3,2,1,0:T(8,128)(2,1)S(1)}, bf16[3,3,64,64]{3,2,1,0:T(8,128)(2,1)}, u32[]{:S(2)}) copy-start(bf16[3,3,64,64]{3,2,1,0:T(8,128)(2,1)} %param.28) | copy-start | bytes 221188
  403.2 180.6 %copy-start.21 = (f32[8,512]{1,0:T(8,128)S(1)}, f32[8,512]{1,0:T(8,128)}, u32[]{:S(2)}) copy-start(f32[8,512]{1,0:T(8,128)} %param.29) | copy-start | bytes 49156
  403.2 92.3 %reduce-scatter.8.cloned.1.call-start = ((), (), s32[]{:S(2)}) async-start(), calls=%async_computation.10 | async-start | bytes 884736 | tf_op jit(solution)/shard_map/reduce_scatter | solution.py:193
  435.9 132.9 %all-reduce.4.cloned.1.call-start = ((), (), s32[]{:S(2)}) async-start(), calls=%async_computation.11 | async-start | bytes 368640 | tf_op jit(solution)/shard_map/psum | solution.py:239
  457.1 127.3 %copy-start.7 = (bf16[512,384]{1,0:T(8,128)(2,1)}, bf16[512,384]{1,0:T(8,128)(2,1)S(1)}, u32[]{:S(2)}) copy-start(bf16[512,384]{1,0:T(8,128)(2,1)S(1)} %get-tuple-element.240) | copy-start | bytes 1179652
  495.5 82.5 %collective-permute-start = (f32[64,384]{1,0:T(8,128)}, f32[64,384]{1,0:T(8,128)S(1)}, u32[]{:S(2)}, u32[]{:S(2)}) collective-permute-start(f32[64,384]{1,0:T(8,128)} %reduce-scatter.8.cloned.1.call-done), channel_id=1, source_target_pairs={{0,0},{1,8},{2,16},{3,24},{4,32},{5,40},{6,48},{7,56},{8,1},{9,9},... | collective-permute-start | bytes 294920 | tf_op jit(solution)/shard_map/ppermute | solution.py:198
  572.0 6.9 %collective-permute-start.1 = (bf16[1,4096]{1,0:T(2,128)(2,1)S(1)}, bf16[1,4096]{1,0:T(2,128)(2,1)S(1)}, u32[]{:S(2)}, u32[]{:S(2)}) collective-permute-start(bf16[1,4096]{1,0:T(2,128)(2,1)S(1)} %slice.193), channel_id=1, source_target_pairs={{0,8},{8,16},{16,24},{24,32},{32,40},{40,48},{48,56},{1,9},{9,17},... | collective-permute-start | bytes 24584 | tf_op jit(solution)/shard_map/ppermute | solution.py:18
  574.6 7.7 %collective-permute-start.2 = (bf16[1,4096]{1,0:T(2,128)(2,1)S(1)}, bf16[1,4096]{1,0:T(2,128)(2,1)S(1)}, u32[]{:S(2)}, u32[]{:S(2)}) collective-permute-start(bf16[1,4096]{1,0:T(2,128)(2,1)S(1)} %slice.195), channel_id=1, source_target_pairs={{8,0},{16,8},{24,16},{32,24},{40,32},{48,40},{56,48},{9,1},{17,9},... | collective-permute-start | bytes 24584 | tf_op jit(solution)/shard_map/ppermute | solution.py:21
  583.8 0.6 copy-start.19
Sparse Core Ops, SparseCore 0:
  44.7 64.2 reduce-scatter.5
  191.0 48.4 all-gather.9
  241.3 48.4 all-gather.11
  291.4 44.1 all-gather.13
Sparse Core Ops, SparseCore 1:
  46.9 50.9 all-gather.5
  99.5 77.4 all-gather.7
  403.3 52.3 reduce-scatter.9
  458.2 37.3 reduce-scatter.7
  498.3 70.5 all-reduce.3
where the time goes:
time: 594 us; the launch traced here: 592 us
  waiting for transfers between devices  344 us (58%)
  matrix products  73.2 us (12%)
  blocking collectives  50 us (8%)
  other arithmetic  49.9 us (8%)
  local copies, waits for them, and re-layouts  40.5 us (7%)
  between operations  17.5 us (3%)
  starting transfers between devices  16 us (3%)
    psum x1, waiting for transfers between devices, per_device(): packed = lax.psum(packed, 'tp')  69.3 us
    all_gather x1, waiting for transfers between devices, per_device(): lax.all_gather(img_qkv, 'seq', axis=0, tiled=True)  61.8 us
    reduce_scatter x1, waiting for transfers between devices, per_device(): lax.psum_scatter(add_rows(txt_norm_rows, txt_qkv), 'seq', scatter_dimensi...  57.2 us
    all_gather x1, waiting for transfers between devices, per_device(): value_piece = lax.all_gather(values_local, 'seq', axis=0, tiled=True)  50.3 us
    all_gather x1, waiting for transfers between devices, per_device(): key_piece = lax.all_gather(keys_local, 'seq', axis=0, tiled=True)  43.4 us
    reduce_scatter x1, waiting for transfers between devices, per_device(): lax.psum_scatter(txt_term.astype(jnp.bfloat16).astype(jnp.float32), 'tp',...  34.9 us
    dot_general x8, matrix products, advance(): jnp.einsum('hqk,khd->hqd', weights.astype(jnp.bfloat16), value_block, pre...  33 us
    all_gather x1, blocking collectives, per_device(): lax.all_gather(txt_attn, 'seq', axis=0, tiled=True)  31.2 us
  transfers between devices with their start and end apart: 13, of which 9 were waited for; matrix products, arithmetic and copies ran while one was open for 23% of the time, Pallas kernels for 0%

commit v1 on v0

--- a/solution.py
+++ b/solution.py
@@ -8,6 +8,13 @@
 EPS = 1e-06
 SHIFT_MU = 1.15
 THETA = 10000.0
+
+
+def all_by_exchange(value, mesh_axis, dim):
+    devices = lax.axis_size(mesh_axis)
+    blocks = jnp.stack([value for _ in range(devices)])
+    blocks = lax.all_to_all(blocks, mesh_axis, split_axis=0, concat_axis=0)
+    return jnp.concatenate(blocks, axis=dim)
 
 
 def extended(block, sides, width):
@@ -112,7 +119,7 @@
     full_width = img_full.shape[1]
     img_norm = modulate(img_full, img_mod)
     txt_norm = modulate(txt_full, txt_mod)
-    img_mixed = add_rows(img_norm, lax.all_gather(img_qkv, "seq", axis=0, tiled=True))
+    img_mixed = add_rows(img_norm, all_by_exchange(img_qkv, "seq", 0))
     txt_norm_rows = lax.all_to_all(txt_norm, "seq", 1, 0, tiled=True)
     txt_mixed = lax.psum_scatter(
         add_rows(txt_norm_rows, txt_qkv), "seq", scatter_dimension=0, tiled=True

time: 594 us -> 603 us (1.015)
  local copies, waits for them, and re-layouts: 40.5 us -> 56.5 us
  waiting for transfers between devices: 344 us -> 331 us
  starting transfers between devices: 16 us -> 22.7 us
    all_gather x1 -> x0, waiting for transfers between devices: 61.8 us -> none  [per_device(): lax.all_gather(img_qkv, 'seq', axis=0, tiled=True)]
    reduce_scatter x1, waiting for transfers between devices: 57.2 us -> 92.8 us  [per_device(): lax.psum_scatter(add_rows(txt_norm_rows, txt_qkv), 'seq', scatter_dimensi...]
    all_to_all x0 -> x1, waiting for transfers between devices: none -> 15.8 us  [all_by_exchange(): blocks = lax.all_to_all(blocks, mesh_axis, split_axis=0, concat_axis=0)]
    all_to_all x0 -> x1, local copies, waits for them, and re-layouts: none -> 7.23 us  [all_by_exchange(): blocks = lax.all_to_all(blocks, mesh_axis, split_axis=0, concat_axis=0)]
    all_to_all x0 -> x1, starting transfers between devices: none -> 6.98 us  [all_by_exchange(): blocks = lax.all_to_all(blocks, mesh_axis, split_axis=0, concat_axis=0)]
    unnamed x50 -> x55, local copies, waits for them, and re-layouts: 11.5 us -> 16.4 us
    unnamed x10 -> x9, waiting for transfers between devices: 19.6 us -> 19.4 us
where the time goes in v1:
time: 603 us; the launch traced here: 602 us
  waiting for transfers between devices  331 us (55%)
  matrix products  73 us (12%)
  local copies, waits for them, and re-layouts  56.5 us (9%)
  other arithmetic  50 us (8%)
  blocking collectives  50 us (8%)
  starting transfers between devices  22.7 us (4%)
  between operations  17.6 us (3%)
    reduce_scatter x1, waiting for transfers between devices, per_device(): lax.psum_scatter(add_rows(txt_norm_rows, txt_qkv), 'seq', scatter_dimensi...  92.8 us
    psum x1, waiting for transfers between devices, per_device(): packed = lax.psum(packed, 'tp')  69.2 us
    all_gather x1, waiting for transfers between devices, per_device(): value_piece = lax.all_gather(values_local, 'seq', axis=0, tiled=True)  50.3 us
    all_gather x1, waiting for transfers between devices, per_device(): key_piece = lax.all_gather(keys_local, 'seq', axis=0, tiled=True)  41.3 us
    reduce_scatter x1, waiting for transfers between devices, per_device(): lax.psum_scatter(txt_term.astype(jnp.bfloat16).astype(jnp.float32), 'tp',...  34.9 us
    dot_general x8, matrix products, advance(): jnp.einsum('hqk,khd->hqd', weights.astype(jnp.bfloat16), value_block, pre...  32.8 us
    all_gather x1, blocking collectives, per_device(): lax.all_gather(txt_attn, 'seq', axis=0, tiled=True)  31.2 us
    reduce_sum x8, other arithmetic, advance(): running = running * rescale + jnp.sum(weights, -1)  26 us
  transfers between devices with their start and end apart: 13, of which 9 were waited for; matrix products, arithmetic and copies ran while one was open for 23% of the time, Pallas kernels for 0%

profile of v1, /device:TPU:24, one launch (start us, length us, event | category | flops | bytes accessed | tf_op | source)
XLA Modules:
  0.0 601.6 jit_solution(7077696169847333164)
XLA Ops:
  8.0 1.4 fusion.103
  10.2 18.8 %all_gather.18 = bf16[64,3072]{1,0:T(8,128)(2,1)S(1)} all-gather(bf16[64,384]{1,0:T(8,128)(2,1)} %param.18), channel_id=1, replica_groups=mesh['req'=4,'seq'=8,'tp'=8] {'tp'}, dimensions={1}, use_global_device_ids=true | all-gather | bytes 442368 | tf_op jit(solution)/shard_map/all_gather | solution.py:117
  30.4 5.2 all-to-all-start
  35.6 2.5 copy.131
  38.1 4.1 all-to-all-done
  42.2 4.0 stack.14
  46.2 7.0 %all-to-all-start.1 = ((bf16[8,384,3,384]{1,3,2,0:T(8,128)(2,1)}), bf16[8,384,3,384]{1,3,2,0:T(8,128)(2,1)}, u32[]{:S(2)}, u32[]{:S(2)}) async-start(bf16[8,384,3,384]{1,3,2,0:T(8,128)(2,1)} %stack.14), calls=%async_computation.2 | async-start | bytes 14155776 | tf_op jit(solution)/shard_map/all_to_all | solution.py:16
  53.2 2.4 copy.128
  55.6 2.2 fusion.106
  60.8 1.2 fusion.44
  62.7 92.8 %reduce-scatter.6.cloned.1.call-done = f32[64,1152]{1,0:T(8,128)} async-done(((f32[512,1152]{1,0:T(8,128)}), f32[64,1152]{1,0:T(8,128)}) %reduce-scatter.6.cloned.1.call-update) | async-done | bytes 294928 | tf_op jit(solution)/shard_map/reduce_scatter | solution.py:124
  157.3 2.5 convert_reduce_fusion
  161.7 15.8 %all-to-all-done.1 = bf16[8,384,3,384]{1,3,2,0:T(8,128)(2,1)} async-done(((bf16[8,384,3,384]{1,3,2,0:T(8,128)(2,1)}), bf16[8,384,3,384]{1,3,2,0:T(8,128)(2,1)}, u32[]{:S(2)}, u32[]{:S(2)}) %all-to-all-start.1) | async-done | bytes 7077920 | tf_op jit(solution)/shard_map/all_to_all | solution.py:16
  177.5 7.2 %copy.132 = bf16[8,384,3,384]{1,0,3,2:T(8,128)(2,1)S(1)} copy(bf16[8,384,3,384]{1,3,2,0:T(8,128)(2,1)} %all-to-all-done.1) | data formatting | bytes 14155776 | tf_op jit(solution)/shard_map/all_to_all | solution.py:16
  184.8 4.7 copy.161
  189.4 6.4 %fusion.23 = f32[512,3,3,128]{0,3,2,1:T(8,128)S(1)} fusion(bf16[3,3,128,3072]{3,2,1,0:T(8,128)(2,1)} %bitcast.182, bf16[512,3072]{1,0:T(8,128)(2,1)S(1)} %copy-done.1, f32[3072]{0:T(1024)S(1)} %bitcast.198, f32[3072]{0:T(1024)S(1)} %bitcast.197, f32[512]{0:T(512)S(1)} %copy-done.25, f32[512]{0:T(512)S(1)} %broadcast_multiply_fusion.2), kind=kOutput, calls=%fused_computation.34 | convolution fusion | flops 3633315840 | bytes 12611584 | tf_op jit(solution)/shard_map/dot_general | solution.py:89
  199.0 2.1 subtract_convert_fusion
  208.4 41.3 %all-gather.7.cloned.1.call-done = bf16[4608,384]{1,0:T(8,128)(2,1)} async-done(((bf16[576,384]{1,0:T(8,128)(2,1)}), bf16[4608,384]{1,0:T(8,128)(2,1)}) %all-gather.7.cloned.1.call-update) | async-done | bytes 3538960 | tf_op jit(solution)/shard_map/all_gather | solution.py:149
  249.7 50.3 %all-gather.9.cloned.1.call-done = bf16[4608,384]{1,0:T(8,128)(2,1)} async-done(((bf16[576,384]{1,0:T(8,128)(2,1)}), bf16[4608,384]{1,0:T(8,128)(2,1)}) %all-gather.9.cloned.1.call-update) | async-done | bytes 3538960 | tf_op jit(solution)/shard_map/all_gather | solution.py:150
  300.0 103.9 %while.18 = (s32[]{:T(128)}, f32[3,576]{1,0:T(4,128)S(1)}, f32[3,576]{1,0:T(4,128)}, f32[3,576,128]{2,1,0:T(8,128)S(1)}, s32[]{:T(128)}, /*index=5*/bf16[4608,38...) while((s32[]{:T(128)}, f32[3,576]{1,0:T(4,128)S(1)}, ...), condition=%wide.region_12.13_spmd.clone, body=%wide.region_9.12_spmd.clone.sunk | while | flops 521231040 | bytes 18747920 | solution.py:181
  300.7 1.2 constant_dynamic-slice_fusion.7
  302.2 3.1 bitcast_reduce_fusion.2
  305.3 3.2 fusion.133
  308.9 4.1 fusion.135
  313.7 1.3 constant_dynamic-slice_fusion.7
  315.2 3.1 bitcast_reduce_fusion.2
  318.3 3.3 fusion.133
  321.9 4.1 fusion.135
  326.7 1.3 constant_dynamic-slice_fusion.7
  328.3 3.1 bitcast_reduce_fusion.2
  331.4 3.2 fusion.133
  334.9 4.1 fusion.135
  339.8 1.2 constant_dynamic-slice_fusion.7
  341.3 3.1 bitcast_reduce_fusion.2
  344.4 3.2 fusion.133
  347.9 4.1 fusion.135
  352.7 1.2 constant_dynamic-slice_fusion.7
  354.3 3.1 bitcast_reduce_fusion.2
  357.3 3.2 fusion.133
  360.9 4.1 fusion.135
  365.7 1.2 constant_dynamic-slice_fusion.7
  367.2 3.1 bitcast_reduce_fusion.2
  370.3 3.2 fusion.133
  373.9 4.1 fusion.135
  378.7 1.2 constant_dynamic-slice_fusion.7
  380.2 3.1 bitcast_reduce_fusion.2
  383.3 3.2 fusion.133
  386.9 4.1 fusion.135
  391.7 1.2 constant_dynamic-slice_fusion.7
  393.2 3.1 bitcast_reduce_fusion.2
  396.3 3.2 fusion.133
  399.8 4.1 fusion.135
  406.8 3.6 convolution_convert_fusion
  410.4 2.8 copy.154
  413.5 31.2 %all_gather.23 = bf16[512,384]{1,0:T(8,128)(2,1)S(1)} all-gather(bf16[64,384]{1,0:T(8,128)(2,1)S(1)} %copy.152), channel_id=1, replica_groups=mesh['req'=4,'seq'=8,'tp'=8] {'seq'}, dimensions={0}, use_global_device_ids=true | all-gather | bytes 442368 | tf_op jit(solution)/shard_map/all_gather | solution.py:196
  444.7 1.3 fusion.29
  447.2 18.3 %reduce-scatter.10.cloned.1.call-done = bf16[384,512]{1,0:T(8,128)(2,1)} async-done(((bf16[3072,512]{1,0:T(8,128)(2,1)}), bf16[384,512]{1,0:T(8,128)(2,1)}) %reduce-scatter.10.cloned.1.call-update) | async-done | bytes 393232
  465.5 1.2 copy.155
  470.5 34.9 %reduce-scatter.8.cloned.1.call-done = f32[64,384]{1,0:T(8,128)} async-done(((f32[512,384]{1,0:T(8,128)}), f32[64,384]{1,0:T(8,128)}) %reduce-scatter.8.cloned.1.call-update) | async-done | bytes 98320 | tf_op jit(solution)/shard_map/reduce_scatter | solution.py:200
  505.4 4.1 collective-permute-start
  509.5 69.2 %all-reduce.4.cloned.1.call-done = f32[514,66]{0,1:T(8,128)} async-done(((f32[514,66]{0,1:T(8,128)}), f32[514,66]{0,1:T(8,128)}) %all-reduce.4.cloned.1.call-update) | async-done | bytes 135712 | tf_op jit(solution)/shard_map/psum | solution.py:246
  581.8 2.5 collective-permute-start.1
  584.5 3.4 collective-permute-start.2
  588.9 3.4 collective-permute-done.2
  (247 shorter events, 42.2 us)
Async XLA Ops:
  8.0 436.7 %copy-start = (bf16[384,384]{1,0:T(8,128)(2,1)S(1)}, bf16[384,384]{1,0:T(8,128)(2,1)}, u32[]{:S(2)}) copy-start(bf16[384,384]{1,0:T(8,128)(2,1)} %param.25) | copy-start | bytes 884740
  30.4 11.8 %all-to-all-start = ((bf16[64,8,384]{2,0,1:T(8,128)(2,1)}), bf16[64,8,384]{2,0,1:T(8,128)(2,1)S(1)}, u32[]{:S(2)}, u32[]{:S(2)}) async-start(bf16[64,8,384]{2,0,1:T(8,128)(2,1)} %bitcast.159), calls=%async_computation | async-start | bytes 786432 | tf_op jit(solution)/shard_map/all_to_all | solution.py:123
  46.2 7.0 %copy-start.8 = (bf16[384,3,384]{2,0,1:T(8,128)(2,1)S(1)}, bf16[384,3,384]{2,0,1:T(8,128)(2,1)}, u32[]{:S(2)}) copy-start(bf16[384,3,384]{2,0,1:T(8,128)(2,1)} %param.22) | copy-start | bytes 2654212
  46.2 131.3 %all-to-all-start.1 = ((bf16[8,384,3,384]{1,3,2,0:T(8,128)(2,1)}), bf16[8,384,3,384]{1,3,2,0:T(8,128)(2,1)}, u32[]{:S(2)}, u32[]{:S(2)}) async-start(bf16[8,384,3,384]{1,3,2,0:T(8,128)(2,1)} %stack.14), calls=%async_computation.2 | async-start | bytes 14155776 | tf_op jit(solution)/shard_map/all_to_all | solution.py:16
  53.2 5.5 copy-start.18
  53.2 5.5 copy-start.24
  53.2 102.3 %reduce-scatter.6.cloned.1.call-start = ((), (), s32[]{:S(2)}) async-start(), calls=%async_computation.5 | async-start | bytes 2654208 | tf_op jit(solution)/shard_map/reduce_scatter | solution.py:124
  57.8 99.5 %all-gather.5.cloned.1.call-start = ((), (), s32[]{:S(2)}) async-start(), calls=%async_computation.6 | async-start | bytes 3538944 | tf_op jit(solution)/shard_map/all_gather | solution.py:116
  58.4 191.3 %all-gather.7.cloned.1.call-start = ((), (), s32[]{:S(2)}) async-start(), calls=%async_computation.7 | async-start | bytes 3981312 | tf_op jit(solution)/shard_map/all_gather | solution.py:149
  156.6 0.7 copy-start.3
  157.3 2.8 copy-start.1
  184.7 4.7 copy-start.22
  184.8 4.7 copy-start.25
  195.8 1.4 copy-start.5
  195.9 2.4 copy-start.16
  195.9 2.7 copy-start.17
  195.9 3.1 copy-start.9
  195.9 3.1 copy-start.10
  198.6 4.8 copy-start.4
  201.1 5.5 copy-start.23
  203.4 96.7 %all-gather.9.cloned.1.call-start = ((), (), s32[]{:S(2)}) async-start(), calls=%async_computation.8 | async-start | bytes 3981312 | tf_op jit(solution)/shard_map/all_gather | solution.py:150
  205.7 201.1 %all-gather.11.cloned.1.call-start = ((), (), s32[]{:S(2)}) async-start(), calls=%async_computation.9 | async-start | bytes 2654208 | tf_op jit(solution)/shard_map/all_gather | solution.py:192
  206.3 259.2 %reduce-scatter.10.cloned.1.call-start = ((), (), s32[]{:S(2)}) async-start(), calls=%async_computation.12 | async-start | bytes 3538944
  302.2 6.4 %copy-start.12 = (f32[3,576]{1,0:T(4,128)S(1)}, f32[3,576]{1,0:T(4,128)}, u32[]{:S(2)}) copy-start(f32[3,576]{1,0:T(4,128)} %get-tuple-element.363) | copy-start | bytes 20740 | tf_op jit(solution)/shard_map/while
  308.6 4.4 copy-start.13
  315.2 6.4 %copy-start.12 = (f32[3,576]{1,0:T(4,128)S(1)}, f32[3,576]{1,0:T(4,128)}, u32[]{:S(2)}) copy-start(f32[3,576]{1,0:T(4,128)} %get-tuple-element.363) | copy-start | bytes 20740 | tf_op jit(solution)/shard_map/while
  321.6 4.4 copy-start.13
  328.2 6.4 %copy-start.12 = (f32[3,576]{1,0:T(4,128)S(1)}, f32[3,576]{1,0:T(4,128)}, u32[]{:S(2)}) copy-start(f32[3,576]{1,0:T(4,128)} %get-tuple-element.363) | copy-start | bytes 20740 | tf_op jit(solution)/shard_map/while
  334.6 4.4 copy-start.13
  341.3 6.4 %copy-start.12 = (f32[3,576]{1,0:T(4,128)S(1)}, f32[3,576]{1,0:T(4,128)}, u32[]{:S(2)}) copy-start(f32[3,576]{1,0:T(4,128)} %get-tuple-element.363) | copy-start | bytes 20740 | tf_op jit(solution)/shard_map/while
  347.7 4.4 copy-start.13
  354.2 6.4 %copy-start.12 = (f32[3,576]{1,0:T(4,128)S(1)}, f32[3,576]{1,0:T(4,128)}, u32[]{:S(2)}) copy-start(f32[3,576]{1,0:T(4,128)} %get-tuple-element.363) | copy-start | bytes 20740 | tf_op jit(solution)/shard_map/while
  360.6 4.4 copy-start.13
  367.2 6.4 %copy-start.12 = (f32[3,576]{1,0:T(4,128)S(1)}, f32[3,576]{1,0:T(4,128)}, u32[]{:S(2)}) copy-start(f32[3,576]{1,0:T(4,128)} %get-tuple-element.363) | copy-start | bytes 20740 | tf_op jit(solution)/shard_map/while
  373.6 4.4 copy-start.13
  380.2 6.4 %copy-start.12 = (f32[3,576]{1,0:T(4,128)S(1)}, f32[3,576]{1,0:T(4,128)}, u32[]{:S(2)}) copy-start(f32[3,576]{1,0:T(4,128)} %get-tuple-element.363) | copy-start | bytes 20740 | tf_op jit(solution)/shard_map/while
  386.6 4.4 copy-start.13
  393.2 6.4 %copy-start.12 = (f32[3,576]{1,0:T(4,128)S(1)}, f32[3,576]{1,0:T(4,128)}, u32[]{:S(2)}) copy-start(f32[3,576]{1,0:T(4,128)} %get-tuple-element.363) | copy-start | bytes 20740 | tf_op jit(solution)/shard_map/while
  399.6 4.4 copy-start.13
  405.1 0.8 copy-start.2
  410.4 2.9 slice-start
  413.3 32.8 %copy-start.20 = (bf16[2,3072]{1,0:T(2,128)(2,1)S(1)}, bf16[2,3072]{1,0:T(2,128)(2,1)}, u32[]{:S(2)}) copy-start(bf16[2,3072]{1,0:T(2,128)(2,1)} %param.26) | copy-start | bytes 36868
  413.3 32.8 %copy-start.11 = (bf16[384,64]{0,1:T(8,128)(2,1)S(1)}, bf16[384,64]{0,1:T(8,128)(2,1)}, u32[]{:S(2)}) copy-start(bf16[384,64]{0,1:T(8,128)(2,1)} %param.27) | copy-start | bytes 147460
  413.3 53.5 %copy-start.6 = (bf16[512,384]{1,0:T(8,128)(2,1)S(1)}, bf16[512,384]{1,0:T(8,128)(2,1)}, u32[]{:S(2)}) copy-start(bf16[512,384]{1,0:T(8,128)(2,1)} %param.17) | copy-start | bytes 1179652
  413.3 174.6 %copy-start.14 = (bf16[64,384]{1,0:T(8,128)(2,1)S(1)}, bf16[64,384]{1,0:T(8,128)(2,1)}, u32[]{:S(2)}) copy-start(bf16[64,384]{1,0:T(8,128)(2,1)} %param.18) | copy-start | bytes 147460
  413.3 179.1 %copy-start.15 = (bf16[3,3,64,64]{3,2,1,0:T(8,128)(2,1)S(1)}, bf16[3,3,64,64]{3,2,1,0:T(8,128)(2,1)}, u32[]{:S(2)}) copy-start(bf16[3,3,64,64]{3,2,1,0:T(8,128)(2,1)} %param.28) | copy-start | bytes 221188
  413.3 180.3 %copy-start.21 = (f32[8,512]{1,0:T(8,128)S(1)}, f32[8,512]{1,0:T(8,128)}, u32[]{:S(2)}) copy-start(f32[8,512]{1,0:T(8,128)} %param.29) | copy-start | bytes 49156
  413.3 92.1 %reduce-scatter.8.cloned.1.call-start = ((), (), s32[]{:S(2)}) async-start(), calls=%async_computation.10 | async-start | bytes 884736 | tf_op jit(solution)/shard_map/reduce_scatter | solution.py:200
  446.0 132.7 %all-reduce.4.cloned.1.call-start = ((), (), s32[]{:S(2)}) async-start(), calls=%async_computation.11 | async-start | bytes 368640 | tf_op jit(solution)/shard_map/psum | solution.py:246
  467.1 127.2 %copy-start.7 = (bf16[512,384]{1,0:T(8,128)(2,1)}, bf16[512,384]{1,0:T(8,128)(2,1)S(1)}, u32[]{:S(2)}) copy-start(bf16[512,384]{1,0:T(8,128)(2,1)S(1)} %get-tuple-element.248) | copy-start | bytes 1179652
  505.4 82.5 %collective-permute-start = (f32[64,384]{1,0:T(8,128)}, f32[64,384]{1,0:T(8,128)S(1)}, u32[]{:S(2)}, u32[]{:S(2)}) collective-permute-start(f32[64,384]{1,0:T(8,128)} %reduce-scatter.8.cloned.1.call-done), channel_id=1, source_target_pairs={{0,0},{1,8},{2,16},{3,24},{4,32},{5,40},{6,48},{7,56},{8,1},{9,9},... | collective-permute-start | bytes 294920 | tf_op jit(solution)/shard_map/ppermute | solution.py:205
  581.8 6.9 %collective-permute-start.1 = (bf16[1,4096]{1,0:T(2,128)(2,1)S(1)}, bf16[1,4096]{1,0:T(2,128)(2,1)S(1)}, u32[]{:S(2)}, u32[]{:S(2)}) collective-permute-start(bf16[1,4096]{1,0:T(2,128)(2,1)S(1)} %slice.193), channel_id=1, source_target_pairs={{0,8},{8,16},{16,24},{24,32},{32,40},{40,48},{48,56},{1,9},{9,17},... | collective-permute-start | bytes 24584 | tf_op jit(solution)/shard_map/ppermute | solution.py:25
  584.5 7.7 %collective-permute-start.2 = (bf16[1,4096]{1,0:T(2,128)(2,1)S(1)}, bf16[1,4096]{1,0:T(2,128)(2,1)S(1)}, u32[]{:S(2)}, u32[]{:S(2)}) collective-permute-start(bf16[1,4096]{1,0:T(2,128)(2,1)S(1)} %slice.195), channel_id=1, source_target_pairs={{8,0},{16,8},{24,16},{32,24},{40,32},{48,40},{56,48},{9,1},{17,9},... | collective-permute-start | bytes 24584 | tf_op jit(solution)/shard_map/ppermute | solution.py:28
  593.6 0.6 copy-start.19
Sparse Core Ops, SparseCore 0:
  58.0 97.4 reduce-scatter.5
  203.5 46.1 all-gather.6
  251.5 48.4 all-gather.8
  301.7 44.1 all-gather.10
Sparse Core Ops, SparseCore 1:
  60.2 74.2 all-gather.4
  413.4 52.1 reduce-scatter.9
  467.9 37.4 reduce-scatter.7
  508.2 70.4 all-reduce.3
